TPU v7x, 256 devices: a whole 4x4x8 slice. The times are simulated.
256 devices in a mesh: wide: 64 (over x, z, core), narrow: 4 (over y).
Axes of the slice: x: 4, y: 4, z: 8, core: 2. Of those that a mesh axis runs over, the one named last changes fastest.
Arguments:
- attn_heads: bfloat16 [8192, 1536], P('wide', 'narrow'), may hold values from -6 to 6
- w_out: bfloat16 [1536, 1536], P('narrow'), may hold values from -0.21875 to 0.21875
- residual: bfloat16 [8192, 1536], P('wide', 'narrow'), may hold values from -6 to 6
- norm_gain: float32 [1536], replicated, may hold values from 0.1 to 1.9
- route_ids: int32 [8192, 4], P('wide'), may hold values from 0 to 31, all different within a row; in each aligned block of 128 rows (0 to 127, 128 to 255, ...) at most 32 rows name the same one
- route_weight: float32 [8192, 4], P('wide'), may hold values from 0.1 to 1
- row_order: int32 [8192], P('wide'), may hold values from 0 to 8191, as said below
- slot_expert: int32 [64], replicated, may hold values from 0 to 31, as said below
- w_in: bfloat16 [64, 2, 768, 1536], P('wide', None, 'narrow')
- w_down: bfloat16 [64, 768, 1536], P('wide', 'narrow')
Outputs:
- block_out: bfloat16 [8192, 1536], P('wide', 'narrow')
Inputs may be any that keep to these rules, and one draw needn't show every extreme that they name: `route_ids`: each row names 4 different experts; among the 128 rows of one index of wide no expert is named more than 32 times. `row_order`: A permutation of the rows; of the 128 rows of each index of wide, exactly 2 have their initial position among the rows of each index of wide. `slot_expert`: every expert is held by one or more slots; slots holding the same expert hold equal w_in and w_down.
All inputs are finite; a program needn't handle non-finite values.
Results may differ from a plain program's by a relative error of at most 0.017.
Values may be sent and summed in bfloat16 or wider, within the bound.
No kernel may reach another device: no remote copies, remote signals or barrier semaphores. Data moves between devices by JAX's collectives and lax.ppermute only.
A program may use at most 128 MiB of HBM per device.

v0:
```python
import jax
import jax.numpy as jnp
from jax import lax
from jax.sharding import PartitionSpec as P


EXPERTS = 32
CAP = 32


def running_rank(onehot):
    return jnp.sum((jnp.cumsum(onehot, axis=0) - onehot) * onehot, axis=1)


def block(
    attn_heads,
    w_out,
    residual,
    norm_gain,
    route_ids,
    route_weight,
    row_order,
    slot_expert,
    w_in,
    w_down,
):
    row_count = residual.shape[0]
    wide_count = lax.axis_size("wide")
    narrow_count = lax.axis_size("narrow")
    width_local = residual.shape[1]
    model_width = width_local * narrow_count
    me_narrow = lax.axis_index("narrow")

    slot_local = w_in.shape[0]
    def ring(weights):
        return [weights] + [
            lax.ppermute(
                weights,
                "narrow",
                perm=[(i, (i + k) % narrow_count) for i in range(narrow_count)],
            )
            for k in range(1, narrow_count)
        ]

    w_in_all = ring(w_in)
    w_down_all = ring(w_down)

    partial_terms = jnp.dot(attn_heads, w_out, preferred_element_type=jnp.float32)
    partial_terms = partial_terms.astype(jnp.bfloat16).reshape(
        row_count, narrow_count, width_local
    )
    partial_terms = jnp.swapaxes(partial_terms, 0, 1)
    partial_terms = lax.all_to_all(partial_terms, "narrow", split_axis=0, concat_axis=0, tiled=True)
    projected = jnp.sum(partial_terms.astype(jnp.float32), axis=0)
    hidden = (residual.astype(jnp.float32) + projected).astype(jnp.bfloat16)
    hidden_f = hidden.astype(jnp.float32)
    spread = jnp.broadcast_to(hidden[None], (narrow_count, row_count, width_local))
    spread = lax.all_to_all(spread, "narrow", split_axis=0, concat_axis=0, tiled=True)
    whole_rows = jnp.moveaxis(spread, 0, 1).reshape(row_count, model_width)
    whole_rows = whole_rows.astype(jnp.float32)
    mean_sq = jnp.mean(whole_rows * whole_rows, axis=1, keepdims=True)
    normed = (whole_rows * lax.rsqrt(mean_sq + 1e-06) * norm_gain).astype(jnp.bfloat16)

    slot_count = slot_expert.shape[0]
    top_count = route_ids.shape[1]
    band = CAP // narrow_count
    held = (slot_expert[None, :] == jnp.arange(EXPERTS, dtype=jnp.int32)[:, None]).astype(jnp.int32)
    copies = jnp.sum(held, axis=1)
    replica_rank = jnp.cumsum(held, axis=1) - held
    flat_ids = route_ids.reshape(-1)
    choose_expert = (flat_ids[:, None] == jnp.arange(EXPERTS, dtype=jnp.int32)[None, :]).astype(
        jnp.int32
    )
    copy_count = jnp.sum(choose_expert * copies[None, :], axis=1)
    replica = jnp.repeat(row_order, top_count) % copy_count
    held_rows = jnp.sum(choose_expert[:, :, None] * held[None, :, :], axis=1)
    rank_rows = jnp.sum(choose_expert[:, :, None] * replica_rank[None, :, :], axis=1)
    slot_hit = held_rows * (rank_rows == replica[:, None]).astype(jnp.int32)
    slot_index = jnp.sum(slot_hit * jnp.arange(slot_count, dtype=jnp.int32)[None, :], axis=1)
    rank = running_rank(slot_hit)
    position = slot_index * CAP + rank
    send_at = jnp.where(
        rank // band == me_narrow, slot_index * band + rank % band, slot_count * band
    )
    picks = send_at.reshape(row_count, top_count)[None, :, :] == jnp.arange(
        slot_count * band, dtype=jnp.int32
    )[:, None, None]
    picks = jnp.any(picks, axis=2).astype(jnp.bfloat16)
    outgoing = jnp.dot(picks, normed, preferred_element_type=jnp.float32).astype(jnp.bfloat16)
    outgoing = outgoing.reshape(wide_count, slot_local, band, model_width)
    arrived = lax.all_to_all(outgoing, "wide", split_axis=0, concat_axis=0, tiled=True)
    summed = None
    for w_in_k, w_down_k in zip(w_in_all, w_down_all):
        gate_up = jnp.einsum(
            "nscd,sghd->nscgh", arrived, w_in_k, preferred_element_type=jnp.float32
        )
        active = (jax.nn.relu(gate_up[:, :, :, 0]) * gate_up[:, :, :, 1]).astype(jnp.bfloat16)
        piece = jnp.einsum(
            "nsch,shd->nscd", active, w_down_k, preferred_element_type=jnp.float32
        )
        piece = piece.astype(jnp.bfloat16).astype(jnp.float32)
        summed = piece if summed is None else summed + piece
    summed = summed.astype(jnp.bfloat16).reshape(
        wide_count, slot_local, band, narrow_count, width_local
    )
    summed = jnp.moveaxis(summed, 3, 1)
    summed = summed.reshape(wide_count * narrow_count, slot_local, band, width_local)
    returned = lax.all_to_all(
        summed, ("wide", "narrow"), split_axis=0, concat_axis=0, tiled=True
    )
    returned = returned.reshape(wide_count, narrow_count, slot_local, band, width_local)
    returned = jnp.swapaxes(returned, 1, 2)
    expert_out = returned.reshape(slot_count * CAP, width_local)[position]
    weighted = route_weight[:, :, None] * expert_out.reshape(
        row_count, top_count, width_local
    ).astype(jnp.float32)
    mixed = (hidden_f + jnp.sum(weighted, axis=1)).astype(jnp.bfloat16)
    pair_rows = row_count // wide_count
    target_dev = row_order // row_count
    target_place = row_order % row_count
    choose_target = (
        target_dev[:, None] == jnp.arange(wide_count, dtype=jnp.int32)[None, :]
    ).astype(jnp.int32)
    packed_index = target_dev * pair_rows + running_rank(choose_target)
    packed = jnp.zeros((row_count, width_local), jnp.bfloat16).at[packed_index].set(mixed)
    places = jnp.zeros((row_count,), jnp.int32).at[packed_index].set(target_place)
    assert row_count <= 256 and pair_rows <= width_local
    place_row = jnp.zeros((wide_count, 1, width_local), jnp.bfloat16)
    place_row = place_row.at[:, 0, :pair_rows].set(
        places.reshape(wide_count, pair_rows).astype(jnp.bfloat16)
    )
    packed = jnp.concatenate(
        [packed.reshape(wide_count, pair_rows, width_local), place_row], axis=1
    )
    arrived_all = lax.all_to_all(packed, "wide", split_axis=0, concat_axis=0, tiled=True)
    arrived_rows = arrived_all[:, :pair_rows]
    arrived_places = arrived_all[:, pair_rows, :pair_rows].astype(jnp.int32)
    return (
        jnp.zeros((row_count, width_local), jnp.bfloat16)
        .at[arrived_places.reshape(-1)]
        .set(arrived_rows.reshape(row_count, width_local))
    )


def solution(mesh):
    placed = (
        P("wide", "narrow"),
        P("narrow", None),
        P("wide", "narrow"),
        P(),
        P("wide", None),
        P("wide", None),
        P("wide"),
        P(),
        P("wide", None, "narrow", None),
        P("wide", "narrow", None),
    )
    return jax.shard_map(
        block, mesh=mesh, in_specs=placed, out_specs=P("wide", "narrow"), check_vma=False
    )
```

profile of v0, /device:TPU:1, one launch (start us, length us, event | category | flops | bytes accessed | tf_op | source)
XLA Modules:
  0.0 208.8 jit_solution(1699690702517789798)
XLA Ops:
  0.0 1.3 copy-done
  1.3 1.3 convolution_convert_fusion.5
  2.5 0.8 copy.57
  3.3 5.0 %all-to-all-start = ((bf16[4,128,384]{2,1,0:T(8,128)(2,1)}), bf16[4,128,384]{2,1,0:T(8,128)(2,1)S(1)}, u32[]{:S(2)}, u32[]{:S(2)}) async-start(bf16[4,128,384]{2,1,0:T(8,128)(2,1)} %bitcast.141), calls=%async_computation | async-start | bytes 786432 | tf_op jit(solution)/shard_map/all_to_all | solution.py:53
  8.3 0.2 reduce_window_sum.38
  9.2 0.9 multiply_reduce_fusion.1
  10.3 1.2 reduce-window.6
  11.5 0.2 slice_reduce_fusion
  12.2 2.4 %all-to-all-done = bf16[4,128,384]{2,1,0:T(8,128)(2,1)S(1)} async-done(((bf16[4,128,384]{2,1,0:T(8,128)(2,1)}), bf16[4,128,384]{2,1,0:T(8,128)(2,1)S(1)}, u32[]{:S(2)}, u32[]{:S(2)}) %all-to-all-start) | async-done | bytes 393248 | tf_op jit(solution)/shard_map/all_to_all | solution.py:53
  14.8 0.8 broadcast_in_dim.17
  15.6 3.5 %all-to-all-start.1 = ((bf16[4,128,384]{1,2,0:T(8,128)(2,1)}), bf16[4,128,384]{1,2,0:T(8,128)(2,1)S(1)}, u32[]{:S(2)}, u32[]{:S(2)}) async-start(bf16[4,128,384]{1,2,0:T(8,128)(2,1)} %broadcast_in_dim.17), calls=%async_computation.1 | async-start | bytes 786432 | tf_op jit(solution)/shard_map/all_to_all | solution.py:58
  19.3 5.9 %all-to-all-done.1 = bf16[4,128,384]{1,2,0:T(8,128)(2,1)S(1)} async-done(((bf16[4,128,384]{1,2,0:T(8,128)(2,1)}), bf16[4,128,384]{1,2,0:T(8,128)(2,1)S(1)}, u32[]{:S(2)}, u32[]{:S(2)}) %all-to-all-start.1) | async-done | bytes 393248 | tf_op jit(solution)/shard_map/all_to_all | solution.py:58
  25.3 0.2 multiply_reduce_fusion.3
  25.5 0.3 fusion.28
  25.8 1.7 fusion.1
  27.5 15.5 %all-to-all-start.2 = ((bf16[64,1,8,1536]{3,2,1,0:T(8,128)(2,1)}), bf16[64,1,8,1536]{3,2,1,0:T(8,128)(2,1)S(1)}, u32[]{:S(2)}, u32[]{:S(2)}) async-start(bf16[64,1,8,1536]{3,2,1,0:T(8,128)(2,1)} %fusion.1), calls=%async_computation.2 | async-start | bytes 3145728 | tf_op jit(solution)/shard_map/all_to_all | solution.py:91
  43.0 0.4 collective-permute-start
  43.4 1.8 collective-permute-start.2
  45.2 1.2 collective-permute-start.1
  46.4 0.7 collective-permute-start.3
  47.1 1.7 collective-permute-start.4
  48.8 34.0 %all-to-all-done.2 = bf16[64,1,8,1536]{3,2,1,0:T(8,128)(2,1)S(1)} async-done(((bf16[64,1,8,1536]{3,2,1,0:T(8,128)(2,1)}), bf16[64,1,8,1536]{3,2,1,0:T(8,128)(2,1)S(1)}, u32[]{:S(2)}, u32[]{:S(2)}) %all-to-all-start.2) | async-done | bytes 1572896 | tf_op jit(solution)/shard_map/all_to_all | solution.py:91
  82.8 2.3 %fusion.10 = f32[64,1,8,2,192]{4,2,3,0,1:T(8,128)S(1)} fusion(bf16[64,1,8,1536]{3,2,1,0:T(8,128)(2,1)S(1)} %all-to-all-done.2, bf16[1,2,192,1536]{3,2,1,0:T(8,128)(2,1)} %param.20), kind=kOutput, calls=%fused_computation.24 | convolution fusion | flops 603979776 | bytes 3538944 | tf_op jit(solution)/shard_map/nscd,sghd->nscgh/dot_general | solution.py:94
  85.1 1.1 collective-permute-start.5
  86.2 2.3 %fusion.13 = f32[64,1,8,2,192]{4,2,3,0,1:T(8,128)S(1)} fusion(bf16[64,1,8,1536]{3,2,1,0:T(8,128)(2,1)S(1)} %all-to-all-done.2, bf16[1,2,192,1536]{3,2,1,0:T(8,128)(2,1)} %collective-permute-done), kind=kOutput, calls=%fused_computation.25 | convolution fusion | flops 603979776 | bytes 3538944 | tf_op jit(solution)/shard_map/nscd,sghd->nscgh/dot_general | solution.py:94
  88.5 0.6 convolution_convert_fusion.3
  89.1 21.1 %collective-permute-done.1 = bf16[1,192,1536]{2,1,0:T(8,128)(2,1)} collective-permute-done((bf16[1,192,1536]{2,1,0:T(8,128)(2,1)S(1)}, bf16[1,192,1536]{2,1,0:T(8,128)(2,1)}, u32[]{:S(2)}, u32[]{:S(2)}) %collective-permute-start.1) | collective-permute-done | bytes 589856 | tf_op jit(solution)/shard_map/ppermute | solution.py:37
  110.2 1.6 convolution_convert_fusion.2
  111.8 2.3 %fusion.16 = f32[64,1,8,2,192]{4,2,3,0,1:T(8,128)S(1)} fusion(bf16[64,1,8,1536]{3,2,1,0:T(8,128)(2,1)S(1)} %all-to-all-done.2, bf16[1,2,192,1536]{3,2,1,0:T(8,128)(2,1)} %collective-permute-done.2), kind=kOutput, calls=%fused_computation.26 | convolution fusion | flops 603979776 | bytes 3538944 | tf_op jit(solution)/shard_map/nscd,sghd->nscgh/dot_general | solution.py:94
  114.1 7.6 %collective-permute-done.3 = bf16[1,192,1536]{2,1,0:T(8,128)(2,1)} collective-permute-done((bf16[1,192,1536]{2,1,0:T(8,128)(2,1)S(1)}, bf16[1,192,1536]{2,1,0:T(8,128)(2,1)}, u32[]{:S(2)}, u32[]{:S(2)}) %collective-permute-start.3) | collective-permute-done | bytes 589856 | tf_op jit(solution)/shard_map/ppermute | solution.py:37
  121.7 1.6 convolution_convert_fusion.1
  123.4 2.3 %fusion.19 = f32[64,1,8,2,192]{4,2,3,0,1:T(8,128)S(1)} fusion(bf16[64,1,8,1536]{3,2,1,0:T(8,128)(2,1)S(1)} %all-to-all-done.2, bf16[1,2,192,1536]{3,2,1,0:T(8,128)(2,1)} %collective-permute-done.4), kind=kOutput, calls=%fused_computation.27 | convolution fusion | flops 603979776 | bytes 3538944 | tf_op jit(solution)/shard_map/nscd,sghd->nscgh/dot_general | solution.py:94
  125.7 0.8 fusion
  126.5 0.2 fusion.74
  126.6 0.2 pad_maximum_fusion
  126.9 1.3 copy.46
  128.2 15.8 %all-to-all-start.3 = ((bf16[256,1,8,384]{3,2,1,0:T(8,128)(2,1)}), bf16[256,1,8,384]{3,2,1,0:T(8,128)(2,1)S(1)}, u32[]{:S(2)}, u32[]{:S(2)}) async-start(bf16[256,1,8,384]{3,2,1,0:T(8,128)(2,1)} %bitcast.143), calls=%async_computation.3 | async-start | bytes 3145728 | tf_op jit(solution)/shard_map/all_to_all | solution.py:108
  144.2 0.2 reduce_window_sum.37
  144.4 0.2 select_reduce_fusion.1
  144.6 1.0 scatter_custom_fusion.1
  145.7 41.9 %all-to-all-done.3 = bf16[256,1,8,384]{3,2,1,0:T(8,128)(2,1)S(1)} async-done(((bf16[256,1,8,384]{3,2,1,0:T(8,128)(2,1)}), bf16[256,1,8,384]{3,2,1,0:T(8,128)(2,1)S(1)}, u32[]{:S(2)}, u32[]{:S(2)}) %all-to-all-start.3) | async-done | bytes 1572896 | tf_op jit(solution)/shard_map/all_to_all | solution.py:108
  187.7 1.9 gather_fusion
  189.6 0.2 reshape.415
  189.8 0.5 multiply_reduce_fusion.2
  190.3 1.1 scatter_custom_fusion
  191.5 0.2 fusion.50
  191.6 15.1 %all_to_all.25 = bf16[64,3,384]{2,1,0:T(4,128)(2,1)S(1)} all-to-all(bf16[64,3,384]{2,1,0:T(4,128)(2,1)S(1)} %fusion.50), channel_id=1, replica_groups=mesh['wide'=64,'narrow'=4] {'wide'}, dimensions={0} | all-to-all | bytes 294912 | tf_op jit(solution)/shard_map/all_to_all | solution.py:135
  207.1 1.6 scatter_custom_fusion.2
  (57 shorter events, 2.5 us)
Async XLA Ops:
  0.0 1.3 copy-start
  0.0 8.3 %copy-start.4 = (s32[64]{0:T(128)S(1)}, s32[64]{0:T(128)}, u32[]{:S(2)}) copy-start(s32[64]{0:T(128)} %param.19) | copy-start | bytes 772
  0.0 8.7 %copy-start.5 = (s32[128,4]{0,1:T(4,128)S(1)}, s32[128,4]{0,1:T(4,128)}, u32[]{:S(2)}) copy-start(s32[128,4]{0,1:T(4,128)} %param.16) | copy-start | bytes 6148
  0.0 9.0 %copy-start.7 = (s32[128]{0:T(128)S(1)}, s32[128]{0:T(128)}, u32[]{:S(2)}) copy-start(s32[128]{0:T(128)} %param.18) | copy-start | bytes 1540
  3.3 11.3 %all-to-all-start = ((bf16[4,128,384]{2,1,0:T(8,128)(2,1)}), bf16[4,128,384]{2,1,0:T(8,128)(2,1)S(1)}, u32[]{:S(2)}, u32[]{:S(2)}) async-start(bf16[4,128,384]{2,1,0:T(8,128)(2,1)} %bitcast.141), calls=%async_computation | async-start | bytes 786432 | tf_op jit(solution)/shard_map/all_to_all | solution.py:53
  8.3 6.3 %copy-start.2 = (bf16[128,384]{1,0:T(8,128)(2,1)S(1)}, bf16[128,384]{1,0:T(8,128)(2,1)}, u32[]{:S(2)}) copy-start(bf16[128,384]{1,0:T(8,128)(2,1)} %param.14) | copy-start | bytes 294916
  12.2 13.3 %copy-start.3 = (f32[1536]{0:T(1024)S(1)}, f32[1536]{0:T(1024)}, u32[]{:S(2)}) copy-start(f32[1536]{0:T(1024)} %param.15) | copy-start | bytes 18436
  15.6 9.7 %all-to-all-start.1 = ((bf16[4,128,384]{1,2,0:T(8,128)(2,1)}), bf16[4,128,384]{1,2,0:T(8,128)(2,1)S(1)}, u32[]{:S(2)}, u32[]{:S(2)}) async-start(bf16[4,128,384]{1,2,0:T(8,128)(2,1)} %broadcast_in_dim.17), calls=%async_computation.1 | async-start | bytes 786432 | tf_op jit(solution)/shard_map/all_to_all | solution.py:58
  27.5 17.7 %copy-start.1 = (bf16[1,192,1536]{2,1,0:T(8,128)(2,1)S(1)}, bf16[1,192,1536]{2,1,0:T(8,128)(2,1)}, u32[]{:S(2)}) copy-start(bf16[1,192,1536]{2,1,0:T(8,128)(2,1)} %param.21) | copy-start | bytes 1769476
  27.5 55.3 %all-to-all-start.2 = ((bf16[64,1,8,1536]{3,2,1,0:T(8,128)(2,1)}), bf16[64,1,8,1536]{3,2,1,0:T(8,128)(2,1)S(1)}, u32[]{:S(2)}, u32[]{:S(2)}) async-start(bf16[64,1,8,1536]{3,2,1,0:T(8,128)(2,1)} %fusion.1), calls=%async_computation.2 | async-start | bytes 3145728 | tf_op jit(solution)/shard_map/all_to_all | solution.py:91
  43.0 42.0 %collective-permute-start = (bf16[1,2,192,1536]{3,2,1,0:T(8,128)(2,1)}, bf16[1,2,192,1536]{3,2,1,0:T(8,128)(2,1)}, u32[]{:S(2)}, u32[]{:S(2)}) collective-permute-start(bf16[1,2,192,1536]{3,2,1,0:T(8,128)(2,1)} %param.20), channel_id=1, source_target_pairs={{0,1},{1,2},{2,3},{3,0},{4,5},{5,6},{6,7},{7,4},{8,9},{9,10},{10,1... | collective-permute-start | bytes 3538952 | tf_op jit(solution)/shard_map/ppermute | solution.py:37
  43.4 68.4 %collective-permute-start.2 = (bf16[1,2,192,1536]{3,2,1,0:T(8,128)(2,1)}, bf16[1,2,192,1536]{3,2,1,0:T(8,128)(2,1)}, u32[]{:S(2)}, u32[]{:S(2)}) collective-permute-start(bf16[1,2,192,1536]{3,2,1,0:T(8,128)(2,1)} %param.20), channel_id=1, source_target_pairs={{0,2},{1,3},{2,0},{3,1},{4,6},{5,7},{6,4},{7,5},{8,10},{9,11},{10,... | collective-permute-start | bytes 3538952 | tf_op jit(solution)/shard_map/ppermute | solution.py:37
  45.2 65.0 %collective-permute-start.1 = (bf16[1,192,1536]{2,1,0:T(8,128)(2,1)S(1)}, bf16[1,192,1536]{2,1,0:T(8,128)(2,1)}, u32[]{:S(2)}, u32[]{:S(2)}) collective-permute-start(bf16[1,192,1536]{2,1,0:T(8,128)(2,1)S(1)} %copy-done.1), channel_id=1, source_target_pairs={{0,1},{1,2},{2,3},{3,0},{4,5},{5,6},{6,7},{7,4},{8,9},{9,10},{10,1... | collective-permute-start | bytes 1769480 | tf_op jit(solution)/shard_map/ppermute | solution.py:37
  46.4 75.4 %collective-permute-start.3 = (bf16[1,192,1536]{2,1,0:T(8,128)(2,1)S(1)}, bf16[1,192,1536]{2,1,0:T(8,128)(2,1)}, u32[]{:S(2)}, u32[]{:S(2)}) collective-permute-start(bf16[1,192,1536]{2,1,0:T(8,128)(2,1)S(1)} %copy-done.1), channel_id=1, source_target_pairs={{0,2},{1,3},{2,0},{3,1},{4,6},{5,7},{6,4},{7,5},{8,10},{9,11},{10,... | collective-permute-start | bytes 1769480 | tf_op jit(solution)/shard_map/ppermute | solution.py:37
  47.1 76.3 %collective-permute-start.4 = (bf16[1,2,192,1536]{3,2,1,0:T(8,128)(2,1)}, bf16[1,2,192,1536]{3,2,1,0:T(8,128)(2,1)}, u32[]{:S(2)}, u32[]{:S(2)}) collective-permute-start(bf16[1,2,192,1536]{3,2,1,0:T(8,128)(2,1)} %param.20), channel_id=1, source_target_pairs={{0,3},{1,0},{2,1},{3,2},{4,7},{5,4},{6,5},{7,6},{8,11},{9,8},{10,9... | collective-permute-start | bytes 3538952 | tf_op jit(solution)/shard_map/ppermute | solution.py:37
  85.1 40.6 %collective-permute-start.5 = (bf16[1,192,1536]{2,1,0:T(8,128)(2,1)S(1)}, bf16[1,192,1536]{2,1,0:T(8,128)(2,1)S(1)}, u32[]{:S(2)}, u32[]{:S(2)}) collective-permute-start(bf16[1,192,1536]{2,1,0:T(8,128)(2,1)S(1)} %copy-done.1), channel_id=1, source_target_pairs={{0,3},{1,0},{2,1},{3,2},{4,7},{5,4},{6,5},{7,6},{8,11},{9,8},{10,9... | collective-permute-start | bytes 1769480 | tf_op jit(solution)/shard_map/ppermute | solution.py:37
  128.2 15.8 %copy-start.6 = (f32[128,4]{0,1:T(4,128)S(1)}, f32[128,4]{0,1:T(4,128)}, u32[]{:S(2)}) copy-start(f32[128,4]{0,1:T(4,128)} %param.17) | copy-start | bytes 6148
  128.2 59.5 %all-to-all-start.3 = ((bf16[256,1,8,384]{3,2,1,0:T(8,128)(2,1)}), bf16[256,1,8,384]{3,2,1,0:T(8,128)(2,1)S(1)}, u32[]{:S(2)}, u32[]{:S(2)}) async-start(bf16[256,1,8,384]{3,2,1,0:T(8,128)(2,1)} %bitcast.143), calls=%async_computation.3 | async-start | bytes 3145728 | tf_op jit(solution)/shard_map/all_to_all | solution.py:108
where the time goes:
time: 210 us; the launch traced here: 209 us
  waiting for transfers between devices  113 us (54%)
  starting transfers between devices  46.6 us (22%)
  matrix products  16.7 us (8%)
  blocking collectives  15.1 us (7%)
  local copies, waits for them, and re-layouts  10.7 us (5%)
  other arithmetic  6.26 us (3%)
    all_to_all x1, waiting for transfers between devices, block(): lax.all_to_all(summed, ('wide', 'narrow'), split_axis=0, concat_axis=0, t...  41.9 us
    all_to_all x1, waiting for transfers between devices, block(): lax.all_to_all(outgoing, 'wide', split_axis=0, concat_axis=0, tiled=True)  34 us
    ppermute x6, waiting for transfers between devices, ring(): lax.ppermute(weights, 'narrow', perm=[(i, (i + k) % narrow_count) for i i...  28.8 us
    all_to_all x1, starting transfers between devices, block(): lax.all_to_all(summed, ('wide', 'narrow'), split_axis=0, concat_axis=0, t...  15.8 us
    all_to_all x1, starting transfers between devices, block(): lax.all_to_all(outgoing, 'wide', split_axis=0, concat_axis=0, tiled=True)  15.5 us
    all_to_all x1, blocking collectives, block(): lax.all_to_all(packed, 'wide', split_axis=0, concat_axis=0, tiled=True)  15.1 us
    dot_general x4, matrix products, block(): jnp.einsum('nscd,sghd->nscgh', arrived, w_in_k, preferred_element_type=jn...  9.07 us
    ppermute x6, starting transfers between devices, ring(): lax.ppermute(weights, 'narrow', perm=[(i, (i + k) % narrow_count) for i i...  6.87 us
  transfers between devices with their start and end apart: 10, of which 6 were waited for; matrix products, arithmetic and copies ran while one was open for 9% of the time, Pallas kernels for 0%

commit v1 on v0

--- a/solution.py
+++ b/solution.py
@@ -110,7 +110,11 @@
     )
     returned = returned.reshape(wide_count, narrow_count, slot_local, band, width_local)
     returned = jnp.swapaxes(returned, 1, 2)
-    expert_out = returned.reshape(slot_count * CAP, width_local)[position]
+    returned = returned.reshape(slot_count * CAP, width_local)
+    take_rows = (
+        position[:, None] == jnp.arange(slot_count * CAP, dtype=jnp.int32)[None, :]
+    ).astype(jnp.bfloat16)
+    expert_out = jnp.dot(take_rows, returned, preferred_element_type=jnp.float32)
     weighted = route_weight[:, :, None] * expert_out.reshape(
         row_count, top_count, width_local
     ).astype(jnp.float32)
@@ -122,7 +126,10 @@
         target_dev[:, None] == jnp.arange(wide_count, dtype=jnp.int32)[None, :]
     ).astype(jnp.int32)
     packed_index = target_dev * pair_rows + running_rank(choose_target)
-    packed = jnp.zeros((row_count, width_local), jnp.bfloat16).at[packed_index].set(mixed)
+    pack_rows = (
+        packed_index[None, :] == jnp.arange(row_count, dtype=jnp.int32)[:, None]
+    ).astype(jnp.bfloat16)
+    packed = jnp.dot(pack_rows, mixed, preferred_element_type=jnp.float32).astype(jnp.bfloat16)
     places = jnp.zeros((row_count,), jnp.int32).at[packed_index].set(target_place)
     assert row_count <= 256 and pair_rows <= width_local
     place_row = jnp.zeros((wide_count, 1, width_local), jnp.bfloat16)
@@ -135,11 +142,14 @@
     arrived_all = lax.all_to_all(packed, "wide", split_axis=0, concat_axis=0, tiled=True)
     arrived_rows = arrived_all[:, :pair_rows]
     arrived_places = arrived_all[:, pair_rows, :pair_rows].astype(jnp.int32)
-    return (
-        jnp.zeros((row_count, width_local), jnp.bfloat16)
-        .at[arrived_places.reshape(-1)]
-        .set(arrived_rows.reshape(row_count, width_local))
-    )
+    place_rows = (
+        arrived_places.reshape(1, -1) == jnp.arange(row_count, dtype=jnp.int32)[:, None]
+    ).astype(jnp.bfloat16)
+    return jnp.dot(
+        place_rows,
+        arrived_rows.reshape(row_count, width_local),
+        preferred_element_type=jnp.float32,
+    ).astype(jnp.bfloat16)
 
 
 def solution(mesh):

time: 210 us -> 207 us (0.986)
  local copies, waits for them, and re-layouts: 10.7 us -> 6.96 us
  matrix products: 16.7 us -> 19.1 us
    dot_general x0 -> x3, matrix products: none -> 2.3 us  [the longest x1 1.29 us: block(): jnp.dot(take_rows, returned, preferred_element_type=jnp.float32)]
where the time goes in v1:
time: 207 us; the launch traced here: 206 us
  waiting for transfers between devices  113 us (55%)
  starting transfers between devices  46.6 us (23%)
  matrix products  19.1 us (9%)
  blocking collectives  15.1 us (7%)
  local copies, waits for them, and re-layouts  6.96 us (3%)
  other arithmetic  4.67 us (2%)
    all_to_all x1, waiting for transfers between devices, block(): lax.all_to_all(summed, ('wide', 'narrow'), split_axis=0, concat_axis=0, t...  42 us
    all_to_all x1, waiting for transfers between devices, block(): lax.all_to_all(outgoing, 'wide', split_axis=0, concat_axis=0, tiled=True)  34 us
    ppermute x6, waiting for transfers between devices, ring(): lax.ppermute(weights, 'narrow', perm=[(i, (i + k) % narrow_count) for i i...  28.7 us
    all_to_all x1, starting transfers between devices, block(): lax.all_to_all(summed, ('wide', 'narrow'), split_axis=0, concat_axis=0, t...  15.7 us
    all_to_all x1, starting transfers between devices, block(): lax.all_to_all(outgoing, 'wide', split_axis=0, concat_axis=0, tiled=True)  15.5 us
    all_to_all x1, blocking collectives, block(): lax.all_to_all(packed, 'wide', split_axis=0, concat_axis=0, tiled=True)  15.1 us
    dot_general x4, matrix products, block(): jnp.einsum('nscd,sghd->nscgh', arrived, w_in_k, preferred_element_type=jn...  9.09 us
    ppermute x6, starting transfers between devices, ring(): lax.ppermute(weights, 'narrow', perm=[(i, (i + k) % narrow_count) for i i...  6.88 us
  transfers between devices with their start and end apart: 10, of which 6 were waited for; matrix products, arithmetic and copies ran while one was open for 9% of the time, Pallas kernels for 0%

profile of v1, /device:TPU:1, one launch (start us, length us, event | category | flops | bytes accessed | tf_op | source)
XLA Modules:
  0.0 205.8 jit_solution(10980237753365758385)
XLA Ops:
  0.0 1.3 copy-done
  1.3 1.3 convolution_convert_fusion.5
  2.5 0.8 copy.50
  3.3 5.0 %all-to-all-start = ((bf16[4,128,384]{2,1,0:T(8,128)(2,1)}), bf16[4,128,384]{2,1,0:T(8,128)(2,1)S(1)}, u32[]{:S(2)}, u32[]{:S(2)}) async-start(bf16[4,128,384]{2,1,0:T(8,128)(2,1)} %bitcast.153), calls=%async_computation | async-start | bytes 786432 | tf_op jit(solution)/shard_map/all_to_all | solution.py:53
  8.3 0.2 reduce_window_sum.38
  9.2 0.9 multiply_reduce_fusion.1
  10.3 1.2 reduce-window.6
  11.5 0.2 slice_reduce_fusion
  12.3 2.3 %all-to-all-done = bf16[4,128,384]{2,1,0:T(8,128)(2,1)S(1)} async-done(((bf16[4,128,384]{2,1,0:T(8,128)(2,1)}), bf16[4,128,384]{2,1,0:T(8,128)(2,1)S(1)}, u32[]{:S(2)}, u32[]{:S(2)}) %all-to-all-start) | async-done | bytes 393248 | tf_op jit(solution)/shard_map/all_to_all | solution.py:53
  14.8 0.8 broadcast_in_dim.16
  15.6 3.5 %all-to-all-start.1 = ((bf16[4,128,384]{1,2,0:T(8,128)(2,1)}), bf16[4,128,384]{1,2,0:T(8,128)(2,1)S(1)}, u32[]{:S(2)}, u32[]{:S(2)}) async-start(bf16[4,128,384]{1,2,0:T(8,128)(2,1)} %broadcast_in_dim.16), calls=%async_computation.1 | async-start | bytes 786432 | tf_op jit(solution)/shard_map/all_to_all | solution.py:58
  19.2 0.1 fusion.41
  19.3 5.9 %all-to-all-done.1 = bf16[4,128,384]{1,2,0:T(8,128)(2,1)S(1)} async-done(((bf16[4,128,384]{1,2,0:T(8,128)(2,1)}), bf16[4,128,384]{1,2,0:T(8,128)(2,1)S(1)}, u32[]{:S(2)}, u32[]{:S(2)}) %all-to-all-start.1) | async-done | bytes 393248 | tf_op jit(solution)/shard_map/all_to_all | solution.py:58
  25.3 0.2 multiply_reduce_fusion.2
  25.5 0.3 fusion.43
  25.8 1.7 fusion.4
  27.5 15.5 %all-to-all-start.2 = ((bf16[64,1,8,1536]{3,2,1,0:T(8,128)(2,1)}), bf16[64,1,8,1536]{3,2,1,0:T(8,128)(2,1)S(1)}, u32[]{:S(2)}, u32[]{:S(2)}) async-start(bf16[64,1,8,1536]{3,2,1,0:T(8,128)(2,1)} %fusion.4), calls=%async_computation.2 | async-start | bytes 3145728 | tf_op jit(solution)/shard_map/all_to_all | solution.py:91
  43.0 0.4 collective-permute-start
  43.4 1.8 collective-permute-start.2
  45.2 1.2 collective-permute-start.1
  46.4 0.7 collective-permute-start.3
  47.1 1.7 collective-permute-start.4
  48.8 34.0 %all-to-all-done.2 = bf16[64,1,8,1536]{3,2,1,0:T(8,128)(2,1)S(1)} async-done(((bf16[64,1,8,1536]{3,2,1,0:T(8,128)(2,1)}), bf16[64,1,8,1536]{3,2,1,0:T(8,128)(2,1)S(1)}, u32[]{:S(2)}, u32[]{:S(2)}) %all-to-all-start.2) | async-done | bytes 1572896 | tf_op jit(solution)/shard_map/all_to_all | solution.py:91
  82.8 2.3 %fusion.15 = f32[64,1,8,2,192]{4,2,3,0,1:T(8,128)S(1)} fusion(bf16[64,1,8,1536]{3,2,1,0:T(8,128)(2,1)S(1)} %all-to-all-done.2, bf16[1,2,192,1536]{3,2,1,0:T(8,128)(2,1)} %param.20), kind=kOutput, calls=%fused_computation.26 | convolution fusion | flops 603979776 | bytes 3538944 | tf_op jit(solution)/shard_map/nscd,sghd->nscgh/dot_general | solution.py:94
  85.1 1.2 collective-permute-start.5
  86.2 2.3 %fusion.18 = f32[64,1,8,2,192]{4,2,3,0,1:T(8,128)S(1)} fusion(bf16[64,1,8,1536]{3,2,1,0:T(8,128)(2,1)S(1)} %all-to-all-done.2, bf16[1,2,192,1536]{3,2,1,0:T(8,128)(2,1)} %collective-permute-done), kind=kOutput, calls=%fused_computation.27 | convolution fusion | flops 603979776 | bytes 3538944 | tf_op jit(solution)/shard_map/nscd,sghd->nscgh/dot_general | solution.py:94
  88.5 0.6 convolution_convert_fusion.3
  89.1 21.1 %collective-permute-done.1 = bf16[1,192,1536]{2,1,0:T(8,128)(2,1)} collective-permute-done((bf16[1,192,1536]{2,1,0:T(8,128)(2,1)S(1)}, bf16[1,192,1536]{2,1,0:T(8,128)(2,1)}, u32[]{:S(2)}, u32[]{:S(2)}) %collective-permute-start.1) | collective-permute-done | bytes 589856 | tf_op jit(solution)/shard_map/ppermute | solution.py:37
  110.2 1.6 convolution_convert_fusion.2
  111.8 2.3 %fusion.21 = f32[64,1,8,2,192]{4,2,3,0,1:T(8,128)S(1)} fusion(bf16[64,1,8,1536]{3,2,1,0:T(8,128)(2,1)S(1)} %all-to-all-done.2, bf16[1,2,192,1536]{3,2,1,0:T(8,128)(2,1)} %collective-permute-done.2), kind=kOutput, calls=%fused_computation.28 | convolution fusion | flops 603979776 | bytes 3538944 | tf_op jit(solution)/shard_map/nscd,sghd->nscgh/dot_general | solution.py:94
  114.1 7.6 %collective-permute-done.3 = bf16[1,192,1536]{2,1,0:T(8,128)(2,1)} collective-permute-done((bf16[1,192,1536]{2,1,0:T(8,128)(2,1)S(1)}, bf16[1,192,1536]{2,1,0:T(8,128)(2,1)}, u32[]{:S(2)}, u32[]{:S(2)}) %collective-permute-start.3) | collective-permute-done | bytes 589856 | tf_op jit(solution)/shard_map/ppermute | solution.py:37
  121.7 1.6 convolution_convert_fusion.1
  123.4 2.3 %fusion.24 = f32[64,1,8,2,192]{4,2,3,0,1:T(8,128)S(1)} fusion(bf16[64,1,8,1536]{3,2,1,0:T(8,128)(2,1)S(1)} %all-to-all-done.2, bf16[1,2,192,1536]{3,2,1,0:T(8,128)(2,1)} %collective-permute-done.4), kind=kOutput, calls=%fused_computation.29 | convolution fusion | flops 603979776 | bytes 3538944 | tf_op jit(solution)/shard_map/nscd,sghd->nscgh/dot_general | solution.py:94
  125.7 0.9 fusion.3
  126.6 0.2 fusion.86
  126.7 0.2 pad_maximum_fusion
  127.0 1.3 copy.39
  128.3 15.7 %all-to-all-start.3 = ((bf16[256,1,8,384]{3,2,1,0:T(8,128)(2,1)}), bf16[256,1,8,384]{3,2,1,0:T(8,128)(2,1)S(1)}, u32[]{:S(2)}, u32[]{:S(2)}) async-start(bf16[256,1,8,384]{3,2,1,0:T(8,128)(2,1)} %bitcast.58), calls=%async_computation.3 | async-start | bytes 3145728 | tf_op jit(solution)/shard_map/all_to_all | solution.py:108
  144.2 0.2 reduce_window_sum.37
  144.4 0.2 select_reduce_fusion.1
  144.6 1.0 scatter_custom_fusion
  145.6 0.2 convert_element_type.252
  145.8 42.0 %all-to-all-done.3 = bf16[256,1,8,384]{3,2,1,0:T(8,128)(2,1)S(1)} async-done(((bf16[256,1,8,384]{3,2,1,0:T(8,128)(2,1)}), bf16[256,1,8,384]{3,2,1,0:T(8,128)(2,1)S(1)}, u32[]{:S(2)}, u32[]{:S(2)}) %all-to-all-start.3) | async-done | bytes 1572896 | tf_op jit(solution)/shard_map/all_to_all | solution.py:108
  187.7 1.3 fusion.32
  189.1 0.2 convolution_convert_fusion.7
  189.3 0.2 fusion.65
  189.5 15.1 %all_to_all.25 = bf16[64,3,384]{2,1,0:T(4,128)(2,1)S(1)} all-to-all(bf16[64,3,384]{2,1,0:T(4,128)(2,1)S(1)} %fusion.65), channel_id=1, replica_groups=mesh['wide'=64,'narrow'=4] {'wide'}, dimensions={0} | all-to-all | bytes 294912 | tf_op jit(solution)/shard_map/all_to_all | solution.py:142
  205.0 0.8 convolution_convert_fusion.6
  (53 shorter events, 2.2 us)
Async XLA Ops:
  0.0 1.3 copy-start
  0.0 8.3 %copy-start.4 = (s32[64]{0:T(128)S(1)}, s32[64]{0:T(128)}, u32[]{:S(2)}) copy-start(s32[64]{0:T(128)} %param.19) | copy-start | bytes 772
  0.0 8.7 %copy-start.5 = (s32[128,4]{0,1:T(4,128)S(1)}, s32[128,4]{0,1:T(4,128)}, u32[]{:S(2)}) copy-start(s32[128,4]{0,1:T(4,128)} %param.16) | copy-start | bytes 6148
  0.0 9.0 %copy-start.6 = (s32[128]{0:T(128)S(1)}, s32[128]{0:T(128)}, u32[]{:S(2)}) copy-start(s32[128]{0:T(128)} %param.18) | copy-start | bytes 1540
  3.3 11.3 %all-to-all-start = ((bf16[4,128,384]{2,1,0:T(8,128)(2,1)}), bf16[4,128,384]{2,1,0:T(8,128)(2,1)S(1)}, u32[]{:S(2)}, u32[]{:S(2)}) async-start(bf16[4,128,384]{2,1,0:T(8,128)(2,1)} %bitcast.153), calls=%async_computation | async-start | bytes 786432 | tf_op jit(solution)/shard_map/all_to_all | solution.py:53
  8.3 6.3 %copy-start.2 = (bf16[128,384]{1,0:T(8,128)(2,1)S(1)}, bf16[128,384]{1,0:T(8,128)(2,1)}, u32[]{:S(2)}) copy-start(bf16[128,384]{1,0:T(8,128)(2,1)} %param.14) | copy-start | bytes 294916
  12.3 13.2 %copy-start.3 = (f32[1536]{0:T(1024)S(1)}, f32[1536]{0:T(1024)}, u32[]{:S(2)}) copy-start(f32[1536]{0:T(1024)} %param.15) | copy-start | bytes 18436
  15.6 9.7 %all-to-all-start.1 = ((bf16[4,128,384]{1,2,0:T(8,128)(2,1)}), bf16[4,128,384]{1,2,0:T(8,128)(2,1)S(1)}, u32[]{:S(2)}, u32[]{:S(2)}) async-start(bf16[4,128,384]{1,2,0:T(8,128)(2,1)} %broadcast_in_dim.16), calls=%async_computation.1 | async-start | bytes 786432 | tf_op jit(solution)/shard_map/all_to_all | solution.py:58
  27.5 17.7 %copy-start.1 = (bf16[1,192,1536]{2,1,0:T(8,128)(2,1)S(1)}, bf16[1,192,1536]{2,1,0:T(8,128)(2,1)}, u32[]{:S(2)}) copy-start(bf16[1,192,1536]{2,1,0:T(8,128)(2,1)} %param.21) | copy-start | bytes 1769476
  27.5 55.3 %all-to-all-start.2 = ((bf16[64,1,8,1536]{3,2,1,0:T(8,128)(2,1)}), bf16[64,1,8,1536]{3,2,1,0:T(8,128)(2,1)S(1)}, u32[]{:S(2)}, u32[]{:S(2)}) async-start(bf16[64,1,8,1536]{3,2,1,0:T(8,128)(2,1)} %fusion.4), calls=%async_computation.2 | async-start | bytes 3145728 | tf_op jit(solution)/shard_map/all_to_all | solution.py:91
  43.0 42.0 %collective-permute-start = (bf16[1,2,192,1536]{3,2,1,0:T(8,128)(2,1)}, bf16[1,2,192,1536]{3,2,1,0:T(8,128)(2,1)}, u32[]{:S(2)}, u32[]{:S(2)}) collective-permute-start(bf16[1,2,192,1536]{3,2,1,0:T(8,128)(2,1)} %param.20), channel_id=1, source_target_pairs={{0,1},{1,2},{2,3},{3,0},{4,5},{5,6},{6,7},{7,4},{8,9},{9,10},{10,1... | collective-permute-start | bytes 3538952 | tf_op jit(solution)/shard_map/ppermute | solution.py:37
  43.4 68.4 %collective-permute-start.2 = (bf16[1,2,192,1536]{3,2,1,0:T(8,128)(2,1)}, bf16[1,2,192,1536]{3,2,1,0:T(8,128)(2,1)}, u32[]{:S(2)}, u32[]{:S(2)}) collective-permute-start(bf16[1,2,192,1536]{3,2,1,0:T(8,128)(2,1)} %param.20), channel_id=1, source_target_pairs={{0,2},{1,3},{2,0},{3,1},{4,6},{5,7},{6,4},{7,5},{8,10},{9,11},{10,... | collective-permute-start | bytes 3538952 | tf_op jit(solution)/shard_map/ppermute | solution.py:37
  45.2 65.0 %collective-permute-start.1 = (bf16[1,192,1536]{2,1,0:T(8,128)(2,1)S(1)}, bf16[1,192,1536]{2,1,0:T(8,128)(2,1)}, u32[]{:S(2)}, u32[]{:S(2)}) collective-permute-start(bf16[1,192,1536]{2,1,0:T(8,128)(2,1)S(1)} %copy-done.1), channel_id=1, source_target_pairs={{0,1},{1,2},{2,3},{3,0},{4,5},{5,6},{6,7},{7,4},{8,9},{9,10},{10,1... | collective-permute-start | bytes 1769480 | tf_op jit(solution)/shard_map/ppermute | solution.py:37
  46.4 75.4 %collective-permute-start.3 = (bf16[1,192,1536]{2,1,0:T(8,128)(2,1)S(1)}, bf16[1,192,1536]{2,1,0:T(8,128)(2,1)}, u32[]{:S(2)}, u32[]{:S(2)}) collective-permute-start(bf16[1,192,1536]{2,1,0:T(8,128)(2,1)S(1)} %copy-done.1), channel_id=1, source_target_pairs={{0,2},{1,3},{2,0},{3,1},{4,6},{5,7},{6,4},{7,5},{8,10},{9,11},{10,... | collective-permute-start | bytes 1769480 | tf_op jit(solution)/shard_map/ppermute | solution.py:37
  47.1 76.3 %collective-permute-start.4 = (bf16[1,2,192,1536]{3,2,1,0:T(8,128)(2,1)}, bf16[1,2,192,1536]{3,2,1,0:T(8,128)(2,1)}, u32[]{:S(2)}, u32[]{:S(2)}) collective-permute-start(bf16[1,2,192,1536]{3,2,1,0:T(8,128)(2,1)} %param.20), channel_id=1, source_target_pairs={{0,3},{1,0},{2,1},{3,2},{4,7},{5,4},{6,5},{7,6},{8,11},{9,8},{10,9... | collective-permute-start | bytes 3538952 | tf_op jit(solution)/shard_map/ppermute | solution.py:37
  85.1 40.6 %collective-permute-start.5 = (bf16[1,192,1536]{2,1,0:T(8,128)(2,1)S(1)}, bf16[1,192,1536]{2,1,0:T(8,128)(2,1)S(1)}, u32[]{:S(2)}, u32[]{:S(2)}) collective-permute-start(bf16[1,192,1536]{2,1,0:T(8,128)(2,1)S(1)} %copy-done.1), channel_id=1, source_target_pairs={{0,3},{1,0},{2,1},{3,2},{4,7},{5,4},{6,5},{7,6},{8,11},{9,8},{10,9... | collective-permute-start | bytes 1769480 | tf_op jit(solution)/shard_map/ppermute | solution.py:37
  128.3 59.4 %copy-start.7 = (f32[128,4]{0,1:T(4,128)S(1)}, f32[128,4]{0,1:T(4,128)}, u32[]{:S(2)}) copy-start(f32[128,4]{0,1:T(4,128)} %param.17) | copy-start | bytes 6148
  128.3 59.4 %all-to-all-start.3 = ((bf16[256,1,8,384]{3,2,1,0:T(8,128)(2,1)}), bf16[256,1,8,384]{3,2,1,0:T(8,128)(2,1)S(1)}, u32[]{:S(2)}, u32[]{:S(2)}) async-start(bf16[256,1,8,384]{3,2,1,0:T(8,128)(2,1)} %bitcast.58), calls=%async_computation.3 | async-start | bytes 3145728 | tf_op jit(solution)/shard_map/all_to_all | solution.py:108

commit v2 on v1

--- a/solution.py
+++ b/solution.py
@@ -42,6 +42,7 @@
             for k in range(1, narrow_count)
         ]
 
+    hid_local = w_down.shape[1]
     w_in_all = ring(w_in)
     w_down_all = ring(w_down)
 
@@ -95,15 +96,13 @@
             "nscd,sghd->nscgh", arrived, w_in_k, preferred_element_type=jnp.float32
         )
         active = (jax.nn.relu(gate_up[:, :, :, 0]) * gate_up[:, :, :, 1]).astype(jnp.bfloat16)
+        w_down_cols = w_down_k.reshape(slot_local, hid_local, narrow_count, width_local)
         piece = jnp.einsum(
-            "nsch,shd->nscd", active, w_down_k, preferred_element_type=jnp.float32
+            "nsch,shpd->npscd", active, w_down_cols, preferred_element_type=jnp.float32
         )
         piece = piece.astype(jnp.bfloat16).astype(jnp.float32)
         summed = piece if summed is None else summed + piece
-    summed = summed.astype(jnp.bfloat16).reshape(
-        wide_count, slot_local, band, narrow_count, width_local
-    )
-    summed = jnp.moveaxis(summed, 3, 1)
+    summed = summed.astype(jnp.bfloat16)
     summed = summed.reshape(wide_count * narrow_count, slot_local, band, width_local)
     returned = lax.all_to_all(
         summed, ("wide", "narrow"), split_axis=0, concat_axis=0, tiled=True

time: 207 us -> 218 us (1.053)
  waiting for transfers between devices: 113 us -> 122 us
    ppermute x6, waiting for transfers between devices: 28.7 us -> 72.7 us  [ring(): lax.ppermute(weights, 'narrow', perm=[(i, (i + k) % narrow_count) for i i...]
    all_to_all x1, waiting for transfers between devices: 34 us -> 0.01 us  [block(): lax.all_to_all(outgoing, 'wide', split_axis=0, concat_axis=0, tiled=True)]
  transfers between devices with their start and end apart: 10 -> 10, of which waited for: 6 -> 5; matrix products, arithmetic and copies ran while one was open for 9% -> 9% of each run, Pallas kernels for 0% -> 0%
where the time goes in v2:
time: 218 us; the launch traced here: 217 us
  waiting for transfers between devices  122 us (56%)
  starting transfers between devices  45.6 us (21%)
  matrix products  20 us (9%)
  blocking collectives  15.1 us (7%)
  local copies, waits for them, and re-layouts  8.95 us (4%)
  other arithmetic  5.02 us (2%)
    ppermute x6, waiting for transfers between devices, ring(): lax.ppermute(weights, 'narrow', perm=[(i, (i + k) % narrow_count) for i i...  72.7 us
    all_to_all x1, waiting for transfers between devices, block(): lax.all_to_all(summed, ('wide', 'narrow'), split_axis=0, concat_axis=0, t...  42 us
    all_to_all x1, starting transfers between devices, block(): lax.all_to_all(summed, ('wide', 'narrow'), split_axis=0, concat_axis=0, t...  15.7 us
    all_to_all x1, starting transfers between devices, block(): lax.all_to_all(outgoing, 'wide', split_axis=0, concat_axis=0, tiled=True)  15.7 us
    all_to_all x1, blocking collectives, block(): lax.all_to_all(packed, 'wide', split_axis=0, concat_axis=0, tiled=True)  15.1 us
    dot_general x4, matrix products, block(): jnp.einsum('nscd,sghd->nscgh', arrived, w_in_k, preferred_element_type=jn...  11 us
    ppermute x6, starting transfers between devices, ring(): lax.ppermute(weights, 'narrow', perm=[(i, (i + k) % narrow_count) for i i...  5.73 us
    all_to_all x1, waiting for transfers between devices, block(): lax.all_to_all(spread, 'narrow', split_axis=0, concat_axis=0, tiled=True)  5.31 us
  transfers between devices with their start and end apart: 10, of which 5 were waited for; matrix products, arithmetic and copies ran while one was open for 9% of the time, Pallas kernels for 0%

profile of v2, /device:TPU:1, one launch (start us, length us, event | category | flops | bytes accessed | tf_op | source)
XLA Modules:
  0.0 217.3 jit_solution(12671224105371325049)
XLA Ops:
  0.0 1.3 copy-done
  1.3 1.3 convolution_convert_fusion.1
  2.5 0.8 copy.80
  3.3 5.0 %all-to-all-start = ((bf16[4,128,384]{2,1,0:T(8,128)(2,1)}), bf16[4,128,384]{2,1,0:T(8,128)(2,1)S(1)}, u32[]{:S(2)}, u32[]{:S(2)}) async-start(bf16[4,128,384]{2,1,0:T(8,128)(2,1)} %bitcast.165), calls=%async_computation | async-start | bytes 786432 | tf_op jit(solution)/shard_map/all_to_all | solution.py:54
  8.3 0.2 reduce_window_sum.38
  9.2 0.9 multiply_reduce_fusion.1
  10.3 1.2 reduce-window.6
  11.5 0.2 slice_reduce_fusion
  12.3 2.3 %all-to-all-done = bf16[4,128,384]{2,1,0:T(8,128)(2,1)S(1)} async-done(((bf16[4,128,384]{2,1,0:T(8,128)(2,1)}), bf16[4,128,384]{2,1,0:T(8,128)(2,1)S(1)}, u32[]{:S(2)}, u32[]{:S(2)}) %all-to-all-start) | async-done | bytes 393248 | tf_op jit(solution)/shard_map/all_to_all | solution.py:54
  14.8 0.8 broadcast_in_dim.16
  15.6 3.5 %all-to-all-start.1 = ((bf16[4,128,384]{1,2,0:T(8,128)(2,1)}), bf16[4,128,384]{1,2,0:T(8,128)(2,1)S(1)}, u32[]{:S(2)}, u32[]{:S(2)}) async-start(bf16[4,128,384]{1,2,0:T(8,128)(2,1)} %broadcast_in_dim.16), calls=%async_computation.1 | async-start | bytes 786432 | tf_op jit(solution)/shard_map/all_to_all | solution.py:59
  19.1 0.7 fusion.89
  19.8 0.1 fusion.40
  20.0 5.3 %all-to-all-done.1 = bf16[4,128,384]{1,2,0:T(8,128)(2,1)S(1)} async-done(((bf16[4,128,384]{1,2,0:T(8,128)(2,1)}), bf16[4,128,384]{1,2,0:T(8,128)(2,1)S(1)}, u32[]{:S(2)}, u32[]{:S(2)}) %all-to-all-start.1) | async-done | bytes 393248 | tf_op jit(solution)/shard_map/all_to_all | solution.py:59
  25.3 0.2 multiply_reduce_fusion.2
  25.5 0.3 fusion.42
  25.8 1.7 fusion.3
  27.5 15.7 %all-to-all-start.2 = ((bf16[64,1,8,1536]{3,2,1,0:T(8,128)(2,1)}), bf16[64,1,8,1536]{3,2,1,0:T(8,128)(2,1)}, u32[]{:S(2)}, u32[]{:S(2)}) async-start(bf16[64,1,8,1536]{3,2,1,0:T(8,128)(2,1)} %fusion.3), calls=%async_computation.2 | async-start | bytes 3145728 | tf_op jit(solution)/shard_map/all_to_all | solution.py:92
  43.2 0.4 collective-permute-start
  43.6 1.8 collective-permute-start.2
  45.4 1.2 collective-permute-start.1
  46.5 0.7 collective-permute-start.3
  47.2 1.7 collective-permute-start.5
  48.9 0.1 reshape.401
  49.1 61.1 %collective-permute-done.1 = bf16[1,192,1536]{2,1,0:T(8,128)(2,1)S(1)} collective-permute-done((bf16[1,192,1536]{2,1,0:T(8,128)(2,1)S(1)}, bf16[1,192,1536]{2,1,0:T(8,128)(2,1)S(1)}, u32[]{:S(2)}, u32[]{:S(2)}) %collective-permute-start.1) | collective-permute-done | bytes 589856 | tf_op jit(solution)/shard_map/ppermute | solution.py:37
  110.3 11.5 %collective-permute-done.3 = bf16[1,192,1536]{2,1,0:T(8,128)(2,1)} collective-permute-done((bf16[1,192,1536]{2,1,0:T(8,128)(2,1)S(1)}, bf16[1,192,1536]{2,1,0:T(8,128)(2,1)}, u32[]{:S(2)}, u32[]{:S(2)}) %collective-permute-start.3) | collective-permute-done | bytes 589856 | tf_op jit(solution)/shard_map/ppermute | solution.py:37
  121.9 1.6 reshape.405
  123.5 1.6 reshape.407
  125.1 2.7 %fusion.17 = f32[64,1,8,2,192]{4,2,3,0,1:T(8,128)S(1)} fusion(bf16[64,1,8,1536]{3,2,1,0:T(8,128)(2,1)} %all-to-all-done.2, bf16[1,2,192,1536]{3,2,1,0:T(8,128)(2,1)} %collective-permute-done), kind=kOutput, calls=%fused_computation.25 | convolution fusion | flops 603979776 | bytes 3538944 | tf_op jit(solution)/shard_map/nscd,sghd->nscgh/dot_general | solution.py:95
  127.9 2.7 %fusion.20 = f32[64,1,8,2,192]{4,2,3,0,1:T(8,128)S(1)} fusion(bf16[64,1,8,1536]{3,2,1,0:T(8,128)(2,1)} %all-to-all-done.2, bf16[1,2,192,1536]{3,2,1,0:T(8,128)(2,1)} %collective-permute-done.2), kind=kOutput, calls=%fused_computation.26 | convolution fusion | flops 603979776 | bytes 3538944 | tf_op jit(solution)/shard_map/nscd,sghd->nscgh/dot_general | solution.py:95
  130.6 0.6 convolution_convert_fusion.4
  131.2 0.6 convolution_convert_fusion.3
  131.8 2.7 %fusion.14 = f32[64,1,8,2,192]{4,2,3,0,1:T(8,128)S(1)} fusion(bf16[64,1,8,1536]{3,2,1,0:T(8,128)(2,1)} %all-to-all-done.2, bf16[1,2,192,1536]{3,2,1,0:T(8,128)(2,1)} %param.20), kind=kOutput, calls=%fused_computation.24 | convolution fusion | flops 603979776 | bytes 3538944 | tf_op jit(solution)/shard_map/nscd,sghd->nscgh/dot_general | solution.py:95
  134.5 0.6 convolution_convert_fusion.5
  135.1 2.7 %fusion.23 = f32[64,1,8,2,192]{4,2,3,0,1:T(8,128)S(1)} fusion(bf16[64,1,8,1536]{3,2,1,0:T(8,128)(2,1)} %all-to-all-done.2, bf16[1,2,192,1536]{3,2,1,0:T(8,128)(2,1)} %collective-permute-done.4), kind=kOutput, calls=%fused_computation.27 | convolution fusion | flops 603979776 | bytes 3538944 | tf_op jit(solution)/shard_map/nscd,sghd->nscgh/dot_general | solution.py:95
  137.8 2.1 add_convert_fusion
  139.9 15.7 %all-to-all-start.3 = ((bf16[256,1,8,384]{3,2,1,0:T(8,128)(2,1)}), bf16[256,1,8,384]{3,2,1,0:T(8,128)(2,1)S(1)}, u32[]{:S(2)}, u32[]{:S(2)}) async-start(bf16[256,1,8,384]{3,2,1,0:T(8,128)(2,1)} %bitcast.60), calls=%async_computation.3 | async-start | bytes 3145728 | tf_op jit(solution)/shard_map/all_to_all | solution.py:107
  155.8 0.2 reduce_window_sum.37
  156.0 0.2 select_reduce_fusion.1
  156.2 1.0 scatter_custom_fusion
  157.2 0.2 convert_element_type.252
  157.3 42.0 %all-to-all-done.3 = bf16[256,1,8,384]{3,2,1,0:T(8,128)(2,1)S(1)} async-done(((bf16[256,1,8,384]{3,2,1,0:T(8,128)(2,1)}), bf16[256,1,8,384]{3,2,1,0:T(8,128)(2,1)S(1)}, u32[]{:S(2)}, u32[]{:S(2)}) %all-to-all-start.3) | async-done | bytes 1572896 | tf_op jit(solution)/shard_map/all_to_all | solution.py:107
  199.3 1.3 fusion.31
  200.6 0.2 convolution_convert_fusion.7
  200.8 0.2 fusion.68
  201.0 15.1 %all_to_all.25 = bf16[64,3,384]{2,1,0:T(4,128)(2,1)S(1)} all-to-all(bf16[64,3,384]{2,1,0:T(4,128)(2,1)S(1)} %fusion.68), channel_id=1, replica_groups=mesh['wide'=64,'narrow'=4] {'wide'}, dimensions={0} | all-to-all | bytes 294912 | tf_op jit(solution)/shard_map/all_to_all | solution.py:141
  216.4 0.1 reshape.413
  216.5 0.8 convolution_convert_fusion.6
  (60 shorter events, 2.2 us)
Async XLA Ops:
  0.0 1.3 copy-start
  0.0 8.3 %copy-start.7 = (s32[64]{0:T(128)S(1)}, s32[64]{0:T(128)}, u32[]{:S(2)}) copy-start(s32[64]{0:T(128)} %param.19) | copy-start | bytes 772
  0.0 8.7 %copy-start.8 = (s32[128,4]{0,1:T(4,128)S(1)}, s32[128,4]{0,1:T(4,128)}, u32[]{:S(2)}) copy-start(s32[128,4]{0,1:T(4,128)} %param.16) | copy-start | bytes 6148
  0.0 9.0 %copy-start.9 = (s32[128]{0:T(128)S(1)}, s32[128]{0:T(128)}, u32[]{:S(2)}) copy-start(s32[128]{0:T(128)} %param.18) | copy-start | bytes 1540
  3.3 11.3 %all-to-all-start = ((bf16[4,128,384]{2,1,0:T(8,128)(2,1)}), bf16[4,128,384]{2,1,0:T(8,128)(2,1)S(1)}, u32[]{:S(2)}, u32[]{:S(2)}) async-start(bf16[4,128,384]{2,1,0:T(8,128)(2,1)} %bitcast.165), calls=%async_computation | async-start | bytes 786432 | tf_op jit(solution)/shard_map/all_to_all | solution.py:54
  8.3 6.3 %copy-start.5 = (bf16[128,384]{1,0:T(8,128)(2,1)S(1)}, bf16[128,384]{1,0:T(8,128)(2,1)}, u32[]{:S(2)}) copy-start(bf16[128,384]{1,0:T(8,128)(2,1)} %param.14) | copy-start | bytes 294916
  12.3 13.2 %copy-start.6 = (f32[1536]{0:T(1024)S(1)}, f32[1536]{0:T(1024)}, u32[]{:S(2)}) copy-start(f32[1536]{0:T(1024)} %param.15) | copy-start | bytes 18436
  14.7 0.9 copy-start.1
  15.6 9.7 %all-to-all-start.1 = ((bf16[4,128,384]{1,2,0:T(8,128)(2,1)}), bf16[4,128,384]{1,2,0:T(8,128)(2,1)S(1)}, u32[]{:S(2)}, u32[]{:S(2)}) async-start(bf16[4,128,384]{1,2,0:T(8,128)(2,1)} %broadcast_in_dim.16), calls=%async_computation.1 | async-start | bytes 786432 | tf_op jit(solution)/shard_map/all_to_all | solution.py:59
  27.5 17.9 %copy-start.3 = (bf16[1,192,1536]{2,1,0:T(8,128)(2,1)S(1)}, bf16[1,192,1536]{2,1,0:T(8,128)(2,1)}, u32[]{:S(2)}) copy-start(bf16[1,192,1536]{2,1,0:T(8,128)(2,1)} %param.21) | copy-start | bytes 1769476
  27.5 97.6 %all-to-all-start.2 = ((bf16[64,1,8,1536]{3,2,1,0:T(8,128)(2,1)}), bf16[64,1,8,1536]{3,2,1,0:T(8,128)(2,1)}, u32[]{:S(2)}, u32[]{:S(2)}) async-start(bf16[64,1,8,1536]{3,2,1,0:T(8,128)(2,1)} %fusion.3), calls=%async_computation.2 | async-start | bytes 3145728 | tf_op jit(solution)/shard_map/all_to_all | solution.py:92
  43.2 81.9 %collective-permute-start = (bf16[1,2,192,1536]{3,2,1,0:T(8,128)(2,1)}, bf16[1,2,192,1536]{3,2,1,0:T(8,128)(2,1)}, u32[]{:S(2)}, u32[]{:S(2)}) collective-permute-start(bf16[1,2,192,1536]{3,2,1,0:T(8,128)(2,1)} %param.20), channel_id=1, source_target_pairs={{0,1},{1,2},{2,3},{3,0},{4,5},{5,6},{6,7},{7,4},{8,9},{9,10},{10,1... | collective-permute-start | bytes 3538952 | tf_op jit(solution)/shard_map/ppermute | solution.py:37
  43.6 84.3 %collective-permute-start.2 = (bf16[1,2,192,1536]{3,2,1,0:T(8,128)(2,1)}, bf16[1,2,192,1536]{3,2,1,0:T(8,128)(2,1)}, u32[]{:S(2)}, u32[]{:S(2)}) collective-permute-start(bf16[1,2,192,1536]{3,2,1,0:T(8,128)(2,1)} %param.20), channel_id=1, source_target_pairs={{0,2},{1,3},{2,0},{3,1},{4,6},{5,7},{6,4},{7,5},{8,10},{9,11},{10,... | collective-permute-start | bytes 3538952 | tf_op jit(solution)/shard_map/ppermute | solution.py:37
  45.4 64.8 %collective-permute-start.1 = (bf16[1,192,1536]{2,1,0:T(8,128)(2,1)S(1)}, bf16[1,192,1536]{2,1,0:T(8,128)(2,1)S(1)}, u32[]{:S(2)}, u32[]{:S(2)}) collective-permute-start(bf16[1,192,1536]{2,1,0:T(8,128)(2,1)S(1)} %copy-done.3), channel_id=1, source_target_pairs={{0,1},{1,2},{2,3},{3,0},{4,5},{5,6},{6,7},{7,4},{8,9},{9,10},{10,1... | collective-permute-start | bytes 1769480 | tf_op jit(solution)/shard_map/ppermute | solution.py:37
  46.5 75.3 %collective-permute-start.3 = (bf16[1,192,1536]{2,1,0:T(8,128)(2,1)S(1)}, bf16[1,192,1536]{2,1,0:T(8,128)(2,1)}, u32[]{:S(2)}, u32[]{:S(2)}) collective-permute-start(bf16[1,192,1536]{2,1,0:T(8,128)(2,1)S(1)} %copy-done.3), channel_id=1, source_target_pairs={{0,2},{1,3},{2,0},{3,1},{4,6},{5,7},{6,4},{7,5},{8,10},{9,11},{10,... | collective-permute-start | bytes 1769480 | tf_op jit(solution)/shard_map/ppermute | solution.py:37
  47.2 76.2 %collective-permute-start.5 = (bf16[1,192,1536]{2,1,0:T(8,128)(2,1)S(1)}, bf16[1,192,1536]{2,1,0:T(8,128)(2,1)}, u32[]{:S(2)}, u32[]{:S(2)}) collective-permute-start(bf16[1,192,1536]{2,1,0:T(8,128)(2,1)S(1)} %copy-done.3), channel_id=1, source_target_pairs={{0,3},{1,0},{2,1},{3,2},{4,7},{5,4},{6,5},{7,6},{8,11},{9,8},{10,9... | collective-permute-start | bytes 1769480 | tf_op jit(solution)/shard_map/ppermute | solution.py:37
  110.2 24.9 %collective-permute-start.4 = (bf16[1,2,192,1536]{3,2,1,0:T(8,128)(2,1)}, bf16[1,2,192,1536]{3,2,1,0:T(8,128)(2,1)}, u32[]{:S(2)}, u32[]{:S(2)}) collective-permute-start(bf16[1,2,192,1536]{3,2,1,0:T(8,128)(2,1)} %param.20), channel_id=1, source_target_pairs={{0,3},{1,0},{2,1},{3,2},{4,7},{5,4},{6,5},{7,6},{8,11},{9,8},{10,9... | collective-permute-start | bytes 3538952 | tf_op jit(solution)/shard_map/ppermute | solution.py:37
  139.9 15.7 %copy-start.4 = (s32[128,4]{1,0:T(8,128)S(1)}, s32[128,4]{1,0:T(8,128)}, u32[]{:S(2)}) copy-start(s32[128,4]{1,0:T(8,128)} %get-tuple-element.23) | copy-start | bytes 6148
  139.9 59.4 %copy-start.10 = (f32[128,4]{0,1:T(4,128)S(1)}, f32[128,4]{0,1:T(4,128)}, u32[]{:S(2)}) copy-start(f32[128,4]{0,1:T(4,128)} %param.17) | copy-start | bytes 6148
  139.9 59.4 %all-to-all-start.3 = ((bf16[256,1,8,384]{3,2,1,0:T(8,128)(2,1)}), bf16[256,1,8,384]{3,2,1,0:T(8,128)(2,1)S(1)}, u32[]{:S(2)}, u32[]{:S(2)}) async-start(bf16[256,1,8,384]{3,2,1,0:T(8,128)(2,1)} %bitcast.60), calls=%async_computation.3 | async-start | bytes 3145728 | tf_op jit(solution)/shard_map/all_to_all | solution.py:107
  157.3 43.3 %copy-start.2 = (bf16[128,384]{1,0:T(8,128)(2,1)S(1)}, bf16[128,384]{1,0:T(8,128)(2,1)}, u32[]{:S(2)}) copy-start(bf16[128,384]{1,0:T(8,128)(2,1)} %copy-done.1) | copy-start | bytes 294916

commit v3 on v1

--- a/solution.py
+++ b/solution.py
@@ -103,14 +103,13 @@
     summed = summed.astype(jnp.bfloat16).reshape(
         wide_count, slot_local, band, narrow_count, width_local
     )
-    summed = jnp.moveaxis(summed, 3, 1)
-    summed = summed.reshape(wide_count * narrow_count, slot_local, band, width_local)
+    summed = jnp.moveaxis(summed, 3, 0)
+    summed = summed.reshape(narrow_count * wide_count, slot_local, band, width_local)
     returned = lax.all_to_all(
-        summed, ("wide", "narrow"), split_axis=0, concat_axis=0, tiled=True
+        summed, ("narrow", "wide"), split_axis=0, concat_axis=0, tiled=True
     )
-    returned = returned.reshape(wide_count, narrow_count, slot_local, band, width_local)
-    returned = jnp.swapaxes(returned, 1, 2)
     returned = returned.reshape(slot_count * CAP, width_local)
+    position = (rank // band) * (slot_count * band) + slot_index * band + rank % band
     take_rows = (
         position[:, None] == jnp.arange(slot_count * CAP, dtype=jnp.int32)[None, :]
     ).astype(jnp.bfloat16)

time: 207 us -> 206 us (level)
  no operation moved by 1% of the time
where the time goes in v3:
time: 206 us; the launch traced here: 205 us
  waiting for transfers between devices  113 us (55%)
  starting transfers between devices  46.6 us (23%)
  matrix products  19.1 us (9%)
  blocking collectives  14.7 us (7%)
  local copies, waits for them, and re-layouts  6.69 us (3%)
  other arithmetic  4.43 us (2%)
    all_to_all x1, waiting for transfers between devices, block(): lax.all_to_all(summed, ('narrow', 'wide'), split_axis=0, concat_axis=0, t...  42 us
    all_to_all x1, waiting for transfers between devices, block(): lax.all_to_all(outgoing, 'wide', split_axis=0, concat_axis=0, tiled=True)  34 us
    ppermute x6, waiting for transfers between devices, ring(): lax.ppermute(weights, 'narrow', perm=[(i, (i + k) % narrow_count) for i i...  28.7 us
    all_to_all x1, starting transfers between devices, block(): lax.all_to_all(summed, ('narrow', 'wide'), split_axis=0, concat_axis=0, t...  15.8 us
    all_to_all x1, starting transfers between devices, block(): lax.all_to_all(outgoing, 'wide', split_axis=0, concat_axis=0, tiled=True)  15.5 us
    all_to_all x1, blocking collectives, block(): lax.all_to_all(packed, 'wide', split_axis=0, concat_axis=0, tiled=True)  14.7 us
    dot_general x4, matrix products, block(): jnp.einsum('nscd,sghd->nscgh', arrived, w_in_k, preferred_element_type=jn...  9.09 us
    ppermute x6, starting transfers between devices, ring(): lax.ppermute(weights, 'narrow', perm=[(i, (i + k) % narrow_count) for i i...  6.87 us
  transfers between devices with their start and end apart: 10, of which 6 were waited for; matrix products, arithmetic and copies ran while one was open for 9% of the time, Pallas kernels for 0%

profile of v3, /device:TPU:1, one launch (start us, length us, event | category | flops | bytes accessed | tf_op | source)
XLA Modules:
  0.0 204.9 jit_solution(10932925155344069700)
XLA Ops:
  0.0 1.3 copy-done
  1.3 1.3 convolution_convert_fusion.5
  2.5 0.8 copy.50
  3.3 5.0 %all-to-all-start = ((bf16[4,128,384]{2,1,0:T(8,128)(2,1)}), bf16[4,128,384]{2,1,0:T(8,128)(2,1)S(1)}, u32[]{:S(2)}, u32[]{:S(2)}) async-start(bf16[4,128,384]{2,1,0:T(8,128)(2,1)} %bitcast.156), calls=%async_computation | async-start | bytes 786432 | tf_op jit(solution)/shard_map/all_to_all | solution.py:53
  8.3 0.2 reduce_window_sum.38
  9.2 0.9 multiply_reduce_fusion.1
  10.3 1.2 reduce-window.6
  11.5 0.2 slice_reduce_fusion
  11.8 0.1 fusion.65
  12.2 2.4 %all-to-all-done = bf16[4,128,384]{2,1,0:T(8,128)(2,1)S(1)} async-done(((bf16[4,128,384]{2,1,0:T(8,128)(2,1)}), bf16[4,128,384]{2,1,0:T(8,128)(2,1)S(1)}, u32[]{:S(2)}, u32[]{:S(2)}) %all-to-all-start) | async-done | bytes 393248 | tf_op jit(solution)/shard_map/all_to_all | solution.py:53
  14.8 0.8 broadcast_in_dim.16
  15.6 3.5 %all-to-all-start.1 = ((bf16[4,128,384]{1,2,0:T(8,128)(2,1)}), bf16[4,128,384]{1,2,0:T(8,128)(2,1)S(1)}, u32[]{:S(2)}, u32[]{:S(2)}) async-start(bf16[4,128,384]{1,2,0:T(8,128)(2,1)} %broadcast_in_dim.16), calls=%async_computation.1 | async-start | bytes 786432 | tf_op jit(solution)/shard_map/all_to_all | solution.py:58
  19.2 0.1 fusion.40
  19.3 5.9 %all-to-all-done.1 = bf16[4,128,384]{1,2,0:T(8,128)(2,1)S(1)} async-done(((bf16[4,128,384]{1,2,0:T(8,128)(2,1)}), bf16[4,128,384]{1,2,0:T(8,128)(2,1)S(1)}, u32[]{:S(2)}, u32[]{:S(2)}) %all-to-all-start.1) | async-done | bytes 393248 | tf_op jit(solution)/shard_map/all_to_all | solution.py:58
  25.3 0.2 multiply_reduce_fusion.2
  25.5 0.3 fusion.42
  25.8 1.7 fusion.3
  27.5 15.5 %all-to-all-start.2 = ((bf16[64,1,8,1536]{3,2,1,0:T(8,128)(2,1)}), bf16[64,1,8,1536]{3,2,1,0:T(8,128)(2,1)S(1)}, u32[]{:S(2)}, u32[]{:S(2)}) async-start(bf16[64,1,8,1536]{3,2,1,0:T(8,128)(2,1)} %fusion.3), calls=%async_computation.2 | async-start | bytes 3145728 | tf_op jit(solution)/shard_map/all_to_all | solution.py:91
  43.0 0.4 collective-permute-start
  43.4 1.8 collective-permute-start.2
  45.2 1.2 collective-permute-start.1
  46.4 0.7 collective-permute-start.3
  47.1 1.7 collective-permute-start.4
  48.8 34.0 %all-to-all-done.2 = bf16[64,1,8,1536]{3,2,1,0:T(8,128)(2,1)S(1)} async-done(((bf16[64,1,8,1536]{3,2,1,0:T(8,128)(2,1)}), bf16[64,1,8,1536]{3,2,1,0:T(8,128)(2,1)S(1)}, u32[]{:S(2)}, u32[]{:S(2)}) %all-to-all-start.2) | async-done | bytes 1572896 | tf_op jit(solution)/shard_map/all_to_all | solution.py:91
  82.8 2.3 %fusion.14 = f32[64,1,8,2,192]{4,2,3,0,1:T(8,128)S(1)} fusion(bf16[64,1,8,1536]{3,2,1,0:T(8,128)(2,1)S(1)} %all-to-all-done.2, bf16[1,2,192,1536]{3,2,1,0:T(8,128)(2,1)} %param.20), kind=kOutput, calls=%fused_computation.24 | convolution fusion | flops 603979776 | bytes 3538944 | tf_op jit(solution)/shard_map/nscd,sghd->nscgh/dot_general | solution.py:94
  85.1 1.1 collective-permute-start.5
  86.2 2.3 %fusion.17 = f32[64,1,8,2,192]{4,2,3,0,1:T(8,128)S(1)} fusion(bf16[64,1,8,1536]{3,2,1,0:T(8,128)(2,1)S(1)} %all-to-all-done.2, bf16[1,2,192,1536]{3,2,1,0:T(8,128)(2,1)} %collective-permute-done), kind=kOutput, calls=%fused_computation.25 | convolution fusion | flops 603979776 | bytes 3538944 | tf_op jit(solution)/shard_map/nscd,sghd->nscgh/dot_general | solution.py:94
  88.5 0.6 convolution_convert_fusion.3
  89.1 21.1 %collective-permute-done.1 = bf16[1,192,1536]{2,1,0:T(8,128)(2,1)} collective-permute-done((bf16[1,192,1536]{2,1,0:T(8,128)(2,1)S(1)}, bf16[1,192,1536]{2,1,0:T(8,128)(2,1)}, u32[]{:S(2)}, u32[]{:S(2)}) %collective-permute-start.1) | collective-permute-done | bytes 589856 | tf_op jit(solution)/shard_map/ppermute | solution.py:37
  110.2 1.6 convolution_convert_fusion.2
  111.8 2.3 %fusion.20 = f32[64,1,8,2,192]{4,2,3,0,1:T(8,128)S(1)} fusion(bf16[64,1,8,1536]{3,2,1,0:T(8,128)(2,1)S(1)} %all-to-all-done.2, bf16[1,2,192,1536]{3,2,1,0:T(8,128)(2,1)} %collective-permute-done.2), kind=kOutput, calls=%fused_computation.26 | convolution fusion | flops 603979776 | bytes 3538944 | tf_op jit(solution)/shard_map/nscd,sghd->nscgh/dot_general | solution.py:94
  114.1 7.6 %collective-permute-done.3 = bf16[1,192,1536]{2,1,0:T(8,128)(2,1)} collective-permute-done((bf16[1,192,1536]{2,1,0:T(8,128)(2,1)S(1)}, bf16[1,192,1536]{2,1,0:T(8,128)(2,1)}, u32[]{:S(2)}, u32[]{:S(2)}) %collective-permute-start.3) | collective-permute-done | bytes 589856 | tf_op jit(solution)/shard_map/ppermute | solution.py:37
  121.8 1.6 convolution_convert_fusion.1
  123.4 2.3 %fusion.23 = f32[64,1,8,2,192]{4,2,3,0,1:T(8,128)S(1)} fusion(bf16[64,1,8,1536]{3,2,1,0:T(8,128)(2,1)S(1)} %all-to-all-done.2, bf16[1,2,192,1536]{3,2,1,0:T(8,128)(2,1)} %collective-permute-done.4), kind=kOutput, calls=%fused_computation.27 | convolution fusion | flops 603979776 | bytes 3538944 | tf_op jit(solution)/shard_map/nscd,sghd->nscgh/dot_general | solution.py:94
  125.7 0.9 add_convert_fusion
  126.6 1.3 copy.39
  127.9 15.8 %all-to-all-start.3 = ((bf16[256,1,8,384]{3,2,1,0:T(8,128)(2,1)}), bf16[256,1,8,384]{3,2,1,0:T(8,128)(2,1)S(1)}, u32[]{:S(2)}, u32[]{:S(2)}) async-start(bf16[256,1,8,384]{3,2,1,0:T(8,128)(2,1)} %bitcast.58), calls=%async_computation.3 | async-start | bytes 3145728 | tf_op jit(solution)/shard_map/all_to_all | solution.py:108
  143.8 0.2 reduce_window_sum.37
  144.0 0.2 select_reduce_fusion.1
  144.2 1.0 scatter_custom_fusion
  145.2 0.2 convert_element_type.252
  145.3 42.0 %all-to-all-done.3 = bf16[256,1,8,384]{3,2,1,0:T(8,128)(2,1)S(1)} async-done(((bf16[256,1,8,384]{3,2,1,0:T(8,128)(2,1)}), bf16[256,1,8,384]{3,2,1,0:T(8,128)(2,1)S(1)}, u32[]{:S(2)}, u32[]{:S(2)}) %all-to-all-start.3) | async-done | bytes 1572896 | tf_op jit(solution)/shard_map/all_to_all | solution.py:108
  187.3 1.3 fusion.31
  188.6 0.2 convolution_convert_fusion.7
  188.9 0.2 fusion.64
  189.0 14.7 %all_to_all.25 = bf16[64,3,384]{2,1,0:T(4,128)(2,1)S(1)} all-to-all(bf16[64,3,384]{2,1,0:T(4,128)(2,1)S(1)} %fusion.64), channel_id=1, replica_groups=mesh['wide'=64,'narrow'=4] {'wide'}, dimensions={0} | all-to-all | bytes 294912 | tf_op jit(solution)/shard_map/all_to_all | solution.py:141
  203.9 0.1 reshape.439
  204.1 0.8 convolution_convert_fusion.6
  (50 shorter events, 1.9 us)
Async XLA Ops:
  0.0 1.3 copy-start
  0.0 8.3 %copy-start.4 = (s32[64]{0:T(128)S(1)}, s32[64]{0:T(128)}, u32[]{:S(2)}) copy-start(s32[64]{0:T(128)} %param.19) | copy-start | bytes 772
  0.0 8.7 %copy-start.5 = (s32[128,4]{0,1:T(4,128)S(1)}, s32[128,4]{0,1:T(4,128)}, u32[]{:S(2)}) copy-start(s32[128,4]{0,1:T(4,128)} %param.16) | copy-start | bytes 6148
  0.0 9.0 %copy-start.6 = (s32[128]{0:T(128)S(1)}, s32[128]{0:T(128)}, u32[]{:S(2)}) copy-start(s32[128]{0:T(128)} %param.18) | copy-start | bytes 1540
  3.3 11.3 %all-to-all-start = ((bf16[4,128,384]{2,1,0:T(8,128)(2,1)}), bf16[4,128,384]{2,1,0:T(8,128)(2,1)S(1)}, u32[]{:S(2)}, u32[]{:S(2)}) async-start(bf16[4,128,384]{2,1,0:T(8,128)(2,1)} %bitcast.156), calls=%async_computation | async-start | bytes 786432 | tf_op jit(solution)/shard_map/all_to_all | solution.py:53
  8.3 6.3 %copy-start.2 = (bf16[128,384]{1,0:T(8,128)(2,1)S(1)}, bf16[128,384]{1,0:T(8,128)(2,1)}, u32[]{:S(2)}) copy-start(bf16[128,384]{1,0:T(8,128)(2,1)} %param.14) | copy-start | bytes 294916
  12.2 13.3 %copy-start.3 = (f32[1536]{0:T(1024)S(1)}, f32[1536]{0:T(1024)}, u32[]{:S(2)}) copy-start(f32[1536]{0:T(1024)} %param.15) | copy-start | bytes 18436
  15.6 9.7 %all-to-all-start.1 = ((bf16[4,128,384]{1,2,0:T(8,128)(2,1)}), bf16[4,128,384]{1,2,0:T(8,128)(2,1)S(1)}, u32[]{:S(2)}, u32[]{:S(2)}) async-start(bf16[4,128,384]{1,2,0:T(8,128)(2,1)} %broadcast_in_dim.16), calls=%async_computation.1 | async-start | bytes 786432 | tf_op jit(solution)/shard_map/all_to_all | solution.py:58
  27.5 17.7 %copy-start.1 = (bf16[1,192,1536]{2,1,0:T(8,128)(2,1)S(1)}, bf16[1,192,1536]{2,1,0:T(8,128)(2,1)}, u32[]{:S(2)}) copy-start(bf16[1,192,1536]{2,1,0:T(8,128)(2,1)} %param.21) | copy-start | bytes 1769476
  27.5 55.3 %all-to-all-start.2 = ((bf16[64,1,8,1536]{3,2,1,0:T(8,128)(2,1)}), bf16[64,1,8,1536]{3,2,1,0:T(8,128)(2,1)S(1)}, u32[]{:S(2)}, u32[]{:S(2)}) async-start(bf16[64,1,8,1536]{3,2,1,0:T(8,128)(2,1)} %fusion.3), calls=%async_computation.2 | async-start | bytes 3145728 | tf_op jit(solution)/shard_map/all_to_all | solution.py:91
  43.0 42.0 %collective-permute-start = (bf16[1,2,192,1536]{3,2,1,0:T(8,128)(2,1)}, bf16[1,2,192,1536]{3,2,1,0:T(8,128)(2,1)}, u32[]{:S(2)}, u32[]{:S(2)}) collective-permute-start(bf16[1,2,192,1536]{3,2,1,0:T(8,128)(2,1)} %param.20), channel_id=1, source_target_pairs={{0,1},{1,2},{2,3},{3,0},{4,5},{5,6},{6,7},{7,4},{8,9},{9,10},{10,1... | collective-permute-start | bytes 3538952 | tf_op jit(solution)/shard_map/ppermute | solution.py:37
  43.4 68.4 %collective-permute-start.2 = (bf16[1,2,192,1536]{3,2,1,0:T(8,128)(2,1)}, bf16[1,2,192,1536]{3,2,1,0:T(8,128)(2,1)}, u32[]{:S(2)}, u32[]{:S(2)}) collective-permute-start(bf16[1,2,192,1536]{3,2,1,0:T(8,128)(2,1)} %param.20), channel_id=1, source_target_pairs={{0,2},{1,3},{2,0},{3,1},{4,6},{5,7},{6,4},{7,5},{8,10},{9,11},{10,... | collective-permute-start | bytes 3538952 | tf_op jit(solution)/shard_map/ppermute | solution.py:37
  45.2 65.0 %collective-permute-start.1 = (bf16[1,192,1536]{2,1,0:T(8,128)(2,1)S(1)}, bf16[1,192,1536]{2,1,0:T(8,128)(2,1)}, u32[]{:S(2)}, u32[]{:S(2)}) collective-permute-start(bf16[1,192,1536]{2,1,0:T(8,128)(2,1)S(1)} %copy-done.1), channel_id=1, source_target_pairs={{0,1},{1,2},{2,3},{3,0},{4,5},{5,6},{6,7},{7,4},{8,9},{9,10},{10,1... | collective-permute-start | bytes 1769480 | tf_op jit(solution)/shard_map/ppermute | solution.py:37
  46.4 75.4 %collective-permute-start.3 = (bf16[1,192,1536]{2,1,0:T(8,128)(2,1)S(1)}, bf16[1,192,1536]{2,1,0:T(8,128)(2,1)}, u32[]{:S(2)}, u32[]{:S(2)}) collective-permute-start(bf16[1,192,1536]{2,1,0:T(8,128)(2,1)S(1)} %copy-done.1), channel_id=1, source_target_pairs={{0,2},{1,3},{2,0},{3,1},{4,6},{5,7},{6,4},{7,5},{8,10},{9,11},{10,... | collective-permute-start | bytes 1769480 | tf_op jit(solution)/shard_map/ppermute | solution.py:37
  47.1 76.3 %collective-permute-start.4 = (bf16[1,2,192,1536]{3,2,1,0:T(8,128)(2,1)}, bf16[1,2,192,1536]{3,2,1,0:T(8,128)(2,1)}, u32[]{:S(2)}, u32[]{:S(2)}) collective-permute-start(bf16[1,2,192,1536]{3,2,1,0:T(8,128)(2,1)} %param.20), channel_id=1, source_target_pairs={{0,3},{1,0},{2,1},{3,2},{4,7},{5,4},{6,5},{7,6},{8,11},{9,8},{10,9... | collective-permute-start | bytes 3538952 | tf_op jit(solution)/shard_map/ppermute | solution.py:37
  85.1 40.6 %collective-permute-start.5 = (bf16[1,192,1536]{2,1,0:T(8,128)(2,1)S(1)}, bf16[1,192,1536]{2,1,0:T(8,128)(2,1)S(1)}, u32[]{:S(2)}, u32[]{:S(2)}) collective-permute-start(bf16[1,192,1536]{2,1,0:T(8,128)(2,1)S(1)} %copy-done.1), channel_id=1, source_target_pairs={{0,3},{1,0},{2,1},{3,2},{4,7},{5,4},{6,5},{7,6},{8,11},{9,8},{10,9... | collective-permute-start | bytes 1769480 | tf_op jit(solution)/shard_map/ppermute | solution.py:37
  127.9 59.4 %copy-start.7 = (f32[128,4]{0,1:T(4,128)S(1)}, f32[128,4]{0,1:T(4,128)}, u32[]{:S(2)}) copy-start(f32[128,4]{0,1:T(4,128)} %param.17) | copy-start | bytes 6148
  127.9 59.4 %all-to-all-start.3 = ((bf16[256,1,8,384]{3,2,1,0:T(8,128)(2,1)}), bf16[256,1,8,384]{3,2,1,0:T(8,128)(2,1)S(1)}, u32[]{:S(2)}, u32[]{:S(2)}) async-start(bf16[256,1,8,384]{3,2,1,0:T(8,128)(2,1)} %bitcast.58), calls=%async_computation.3 | async-start | bytes 3145728 | tf_op jit(solution)/shard_map/all_to_all | solution.py:108
